TPU v7x, 256 devices: a whole 4x4x8 slice. The times are simulated.
256 devices in a mesh: req: 64 (over x, z, core), mlp: 4 (over y).
Axes of the slice: x: 4, y: 4, z: 8, core: 2. Of those that a mesh axis runs over, the one named last changes fastest.
Arguments:
- drafts: bfloat16 [512, 16, 2048], P('req', None, 'mlp'), may hold values from -60 to 60
- slot_of: int32 [512], replicated, may hold values from 0 to 511, as said below
- lengths: int32 [512], P('req'), may hold values from 2 to 256, as said below
- parents: int32 [512, 16], P('req'), may hold values from 0 to 14, as said below
- accepted_tokens: int32 [512, 8], P('req'), may hold values from 0 to 15, as said below
- cached_key_value: bfloat16 [512, 256, 4, 128], P('req', None, 'mlp'), may hold values from -2000 to 2000
- attn_gain: float32 [2048], replicated, may hold values from 0.1 to 1.9
- query_weight: bfloat16 [2048, 768], P(None, 'mlp'), may hold values from -0.125 to 0.125
- key_value_weight: bfloat16 [2048, 512], P(None, 'mlp'), may hold values from -0.125 to 0.125
- w_out: bfloat16 [768, 2048], P('mlp'), may hold values from -0.21875 to 0.21875
- mlp_gain: float32 [2048], replicated, may hold values from 0.1 to 1.9
- w_gate: bfloat16 [2048, 2560], P(None, 'mlp'), may hold values from -0.125 to 0.125
- w_up: bfloat16 [2048, 2560], P(None, 'mlp'), may hold values from -0.125 to 0.125
- w_down: bfloat16 [2560, 2048], P('mlp'), may hold values from -0.125 to 0.125
Outputs:
- layer_output: bfloat16 [512, 16, 2048], P('req', None, 'mlp')
- accepted_kv: bfloat16 [512, 8, 4, 128], P('req', None, 'mlp')
Inputs may be any that keep to these rules, and one draw needn't show every extreme that they name: `slot_of`: A permutation of the 512 slots; the cache of slot s is held by index s // 8 of req. Of the 8 requests that arrive on one index of req, at most 1 have their caches on any one index, and that many do for some. `lengths`: some slot holds exactly 256 cached positions. parents[s, 0] = 0 and parents[s, j] < j for j >= 1. accepted_tokens[s, 0] = 0, the entries rise, and each entry is the parent of the next.
All inputs are finite; a program needn't handle non-finite values.
Results may differ from a plain program's by a relative error of at most 0.0095.
Values may be sent and summed in bfloat16 or wider, within the bound.
No kernel may reach another device: no remote copies, remote signals or barrier semaphores. Data moves between devices by JAX's collectives and lax.ppermute only.
A program may use at most 64 MiB of HBM per device.

v0:
```python
import math
import jax
import jax.numpy as jnp
from jax import lax
from jax.sharding import PartitionSpec as P

HEAD_DIM = 64
EPS = 1e-06
HIGH = lax.Precision.HIGHEST


def route_tables(slot_of, per_owner_rows, sources, groups, my_index):
    owners = slot_of // per_owner_rows
    owner_grid = owners.reshape(sources, per_owner_rows)
    request_ids = jnp.arange(per_owner_rows)
    earlier = request_ids[None, :] < request_ids[:, None]
    position = jnp.sum((owner_grid[:, :, None] == owner_grid[:, None, :]) & earlier[None], axis=2)
    column = (jnp.arange(sources, dtype=jnp.int32)[:, None] * groups + position).reshape(-1)
    slot_count = sources * groups
    my_owners = lax.dynamic_index_in_dim(owner_grid, my_index, 0, keepdims=False)
    my_position = lax.dynamic_index_in_dim(position, my_index, 0, keepdims=False)
    target = my_owners * groups + my_position
    sender = (jnp.arange(slot_count)[:, None] == target[None, :]).astype(jnp.bfloat16)
    arrive = (slot_of[None, :] == my_index * per_owner_rows + request_ids[:, None]).astype(
        jnp.bfloat16
    )
    places = (column[:, None] == jnp.arange(slot_count)[None, :]).astype(jnp.bfloat16)
    receiver = jnp.dot(arrive, places, preferred_element_type=jnp.float32).astype(jnp.bfloat16)
    return (sender, receiver)


def ancestry(tree_links, tokens):
    parent_link = (
        tree_links[:, :, None] == jnp.arange(tokens, dtype=jnp.int32)[None, None, :]
    ).astype(jnp.float32)
    reachable = jnp.maximum(parent_link, jnp.eye(tokens, dtype=jnp.float32)[None])
    for squaring in range(max(tokens - 1, 1).bit_length()):
        reachable = jnp.minimum(
            jnp.einsum("rij,rjk->rik", reachable, reachable, precision=HIGH), 1.0
        )
    return reachable > 0.5


def cache_scores(query_rows, cache_block, cache_len, score_scale, head_size):
    key_rows = cache_block[..., :head_size].astype(jnp.float32)
    scores = jnp.einsum("rtkgd,rckd->rkgtc", query_rows, key_rows, precision=HIGH) * score_scale
    row_ids = jnp.arange(cache_block.shape[1])
    live_rows = row_ids[None, :] < cache_len[:, None]
    return jnp.where(live_rows[:, None, None, None, :], scores, -jnp.inf)


def weighted(weights, cache_block, head_size):
    return jnp.einsum(
        "rkgtc,rckd->rtkgd",
        weights,
        cache_block[..., head_size:],
        preferred_element_type=jnp.float32,
    )


def per_device(
    drafts,
    slot_of,
    lengths,
    parents,
    accepted_tokens,
    cached_key_value,
    attn_gain,
    query_weight,
    key_value_weight,
    w_out,
    mlp_gain,
    w_gate,
    w_up,
    w_down,
):
    req_count = lax.axis_size("req")
    my_index = lax.axis_index("req")
    part_index = lax.axis_index("mlp")
    per_owner_rows, tokens, quarter = drafts.shape
    sends = max(1, per_owner_rows // req_count)
    sender, receiver = route_tables(slot_of, per_owner_rows, req_count, sends, my_index)
    flat_rows = drafts.reshape(per_owner_rows, tokens * quarter)
    outgoing = jnp.dot(sender, flat_rows, preferred_element_type=jnp.float32).astype(jnp.bfloat16)
    outgoing = outgoing.reshape(req_count, sends, tokens * quarter)
    incoming = lax.all_to_all(outgoing, "req", split_axis=0, concat_axis=0, tiled=True)
    local_rows = jnp.dot(
        receiver,
        incoming.reshape(req_count * sends, tokens * quarter),
        preferred_element_type=jnp.float32,
    ).astype(jnp.bfloat16)
    local_rows = local_rows.reshape(per_owner_rows * tokens, quarter)
    full_rows = lax.all_gather(local_rows, "mlp", axis=1, tiled=True)
    wide_rows = full_rows.astype(jnp.float32)
    normalized_rows = (
        wide_rows
        * lax.rsqrt(jnp.mean(wide_rows * wide_rows, axis=1, keepdims=True) + EPS)
        * attn_gain
    ).astype(jnp.bfloat16)
    kv_heads = key_value_weight.shape[1] // (2 * HEAD_DIM)
    group_heads = query_weight.shape[1] // (kv_heads * HEAD_DIM)
    query_rows = jnp.dot(normalized_rows, query_weight, preferred_element_type=jnp.float32).reshape(
        per_owner_rows, tokens, kv_heads, group_heads, HEAD_DIM
    )
    new_key_value = (
        jnp.dot(normalized_rows, key_value_weight, preferred_element_type=jnp.float32)
        .astype(jnp.bfloat16)
        .reshape(per_owner_rows, tokens, kv_heads, 2 * HEAD_DIM)
    )
    picker = (
        accepted_tokens[:, :, None] == jnp.arange(tokens, dtype=jnp.int32)[None, None, :]
    ).astype(jnp.bfloat16)
    accepted_rows = jnp.einsum(
        "rat,rtkd->rakd", picker, new_key_value, preferred_element_type=jnp.float32
    ).astype(jnp.bfloat16)
    score_scale = 1.0 / math.sqrt(HEAD_DIM)
    draft_keys = new_key_value[..., :HEAD_DIM].astype(jnp.float32)
    draft_scores = (
        jnp.einsum("rtkgd,rjkd->rkgtj", query_rows, draft_keys, precision=HIGH) * score_scale
    )
    draft_scores = jnp.where(ancestry(parents, tokens)[:, None, None], draft_scores, -jnp.inf)
    draft_top = jnp.max(draft_scores, axis=-1)
    scores = cache_scores(query_rows, cached_key_value, lengths, score_scale, HEAD_DIM)
    row_top = jnp.maximum(draft_top, jnp.max(scores, axis=-1))
    weights = jnp.exp(scores - row_top[..., None]).astype(jnp.bfloat16)
    numerator = weighted(weights, cached_key_value, HEAD_DIM)
    denominator = jnp.sum(weights.astype(jnp.float32), axis=-1)
    draft_weights = jnp.exp(draft_scores - row_top[..., None]).astype(jnp.bfloat16)
    numerator = numerator + jnp.einsum(
        "rkgtj,rjkd->rtkgd",
        draft_weights,
        new_key_value[..., HEAD_DIM:],
        preferred_element_type=jnp.float32,
    )
    denominator = denominator + jnp.sum(draft_weights.astype(jnp.float32), axis=-1)
    attended = (numerator / jnp.transpose(denominator, (0, 3, 1, 2))[..., None]).astype(
        jnp.bfloat16
    )
    attended = attended.reshape(per_owner_rows * tokens, kv_heads * group_heads * HEAD_DIM)
    head_part = jnp.dot(attended, w_out, preferred_element_type=jnp.float32)
    attn_sum = lax.psum(head_part.astype(jnp.bfloat16), "mlp").astype(jnp.float32)
    residual = wide_rows + attn_sum
    normed_two = (
        residual * lax.rsqrt(jnp.mean(residual * residual, axis=1, keepdims=True) + EPS) * mlp_gain
    ).astype(jnp.bfloat16)
    gate_out = jnp.dot(normed_two, w_gate, preferred_element_type=jnp.float32)
    up_out = jnp.dot(normed_two, w_up, preferred_element_type=jnp.float32)
    residual_share = lax.dynamic_slice_in_dim(residual, part_index * quarter, quarter, 1)
    hidden = (jax.nn.silu(gate_out) * up_out).astype(jnp.bfloat16)
    unit_part = jnp.dot(hidden, w_down, preferred_element_type=jnp.float32)
    unit_share = lax.psum_scatter(
        unit_part.astype(jnp.bfloat16), "mlp", scatter_dimension=1, tiled=True
    ).astype(jnp.float32)
    result = (residual_share + unit_share).astype(jnp.bfloat16)
    result_rows = result.reshape(per_owner_rows, tokens * quarter)
    returning = jnp.dot(receiver.T, result_rows, preferred_element_type=jnp.float32).astype(
        jnp.bfloat16
    )
    returning = returning.reshape(req_count, sends, tokens * quarter)
    arrived = lax.all_to_all(returning, "req", split_axis=0, concat_axis=0, tiled=True)
    back_rows = jnp.dot(
        sender.T,
        arrived.reshape(req_count * sends, tokens * quarter),
        preferred_element_type=jnp.float32,
    ).astype(jnp.bfloat16)
    return (back_rows.reshape(per_owner_rows, tokens, quarter), accepted_rows)


def solution(mesh):
    placed = (
        P("req", None, "mlp"),
        P(),
        P("req"),
        P("req", None),
        P("req", None),
        P("req", None, "mlp", None),
        P(),
        P(None, "mlp"),
        P(None, "mlp"),
        P("mlp", None),
        P(),
        P(None, "mlp"),
        P(None, "mlp"),
        P("mlp", None),
    )
    return jax.shard_map(
        per_device,
        mesh=mesh,
        in_specs=placed,
        out_specs=(P("req", None, "mlp"), P("req", None, "mlp", None)),
        check_vma=False,
    )
```

profile of v0, /device:TPU:1, one launch (start us, length us, event | category | flops | bytes accessed | tf_op | source)
XLA Modules:
  0.0 239.9 jit_solution(3685939278999989164)
XLA Ops:
  7.2 0.0 copy-start
  7.2 0.8 add_select_fusion
  8.0 0.1 reshape.195
  8.1 0.1 copy.74
  8.2 1.0 copy.100
  9.2 0.1 convert_reduce_fusion.2
  9.3 0.2 add_reduce_fusion
  9.5 0.5 copy-done.5
  10.0 1.4 fusion
  11.4 0.6 broadcast.99
  12.0 3.4 %reduce.6 = bf16[64,8192]{1,0:T(8,128)(2,1)} reduce(bf16[64,1,8192]{2,0,1:T(8,128)(2,1)} %fusion, bf16[]{:T(256)} %broadcast.99), dimensions={1}, to_apply=%copy.78.reduce_sub_computation | reduce | bytes 2097154 | tf_op jit(solution)/shard_map/reshape | solution.py:85
  15.4 2.7 %reshape.219 = bf16[64,2,4096]{2,1,0:T(2,128)(2,1)} reshape(bf16[64,8192]{1,0:T(8,128)(2,1)} %reduce.6) | data formatting | bytes 2097152
  18.1 13.2 %all-to-all-start = ((bf16[64,2,4096]{2,1,0:T(2,128)(2,1)}), bf16[64,2,4096]{2,1,0:T(2,128)(2,1)}, u32[]{:S(2)}, u32[]{:S(2)}) async-start(bf16[64,2,4096]{2,1,0:T(2,128)(2,1)} %reshape.219), calls=%async_computation | async-start | bytes 2097152 | tf_op jit(solution)/shard_map/all_to_all | solution.py:86
  31.3 0.0 all-reduce.2.cloned.1.call-start
  31.3 0.1 copy.77
  31.4 0.1 add.95
  31.5 0.3 convolution_minimum_fusion.3
  31.8 0.2 convolution_minimum_fusion.2
  32.0 0.2 convolution_minimum_fusion.1
  32.2 0.2 fusion.9
  32.4 0.1 copy.82
  32.5 0.0 copy-done.9
  32.5 0.7 iota_compare_fusion.10
  33.2 0.3 convolution_convert_fusion.8
  33.4 26.3 %all-to-all-done = bf16[64,2,4096]{2,1,0:T(2,128)(2,1)} async-done(((bf16[64,2,4096]{2,1,0:T(2,128)(2,1)}), bf16[64,2,4096]{2,1,0:T(2,128)(2,1)}, u32[]{:S(2)}, u32[]{:S(2)}) %all-to-all-start) | async-done | bytes 1048608 | tf_op jit(solution)/shard_map/all_to_all | solution.py:86
  59.7 7.5 %reshape.220 = bf16[64,1,8192]{2,1,0:T(2,128)(2,1)} reshape(bf16[64,2,4096]{2,1,0:T(2,128)(2,1)} %all-to-all-done) | data formatting | bytes 2097152
  67.2 2.8 %convolution_convert_fusion.3 = bf16[8,8192]{1,0:T(8,128)(2,1)S(1)} fusion(bf16[8,64]{1,0:T(8,128)(2,1)S(1)} %convolution_convert_fusion.8, bf16[64,1,8192]{2,1,0:T(2,128)(2,1)} %reshape.220), kind=kOutput, calls=%fused_computation.5 | convolution fusion | flops 8454144 | bytes 1180672 | tf_op jit(solution)/shard_map/dot_general | solution.py:87
  70.0 0.1 reshape.199
  70.1 11.4 %all_gather.3 = bf16[128,2048]{1,0:T(8,128)(2,1)S(1)} all-gather(bf16[128,512]{1,0:T(8,128)(2,1)S(1)} %reshape.199), channel_id=1, replica_groups=mesh['req'=64,'mlp'=4] {'mlp'}, dimensions={1}, use_global_device_ids=true | all-gather | bytes 655360 | tf_op jit(solution)/shard_map/all_gather | solution.py:93
  81.4 0.2 fusion.13
  81.6 2.0 convolution_convert_fusion.6
  83.7 1.6 fusion.34
  85.2 0.1 reshape.200
  85.4 0.0 copy-start.1
  85.4 1.5 fusion.53
  86.9 1.8 fusion.54
  88.7 0.3 convert_reduce_fusion
  88.9 1.5 convolution_bitcast_fusion
  90.4 0.1 convert_reduce_fusion.1
  90.5 0.0 copy-start.2
  90.5 0.3 fusion.12
  90.8 0.1 copy.86
  90.8 0.1 reshape.208
  91.0 2.2 convolution_convert_fusion.5
  93.2 0.0 all-reduce.2.cloned.1.call-update
  93.2 0.0 reduce-scatter.2.cloned.1.call-start
  93.3 44.9 %all-reduce.2.cloned.1.call-done = bf16[128,2048]{1,0:T(8,128)(2,1)} async-done(((bf16[128,2048]{1,0:T(8,128)(2,1)}), bf16[128,2048]{1,0:T(8,128)(2,1)}) %all-reduce.2.cloned.1.call-update) | async-done | bytes 524304 | tf_op jit(solution)/shard_map/psum | solution.py:141
  138.2 2.2 convert_add_fusion
  140.4 2.5 %fusion.52 = f32[128,640]{1,0:T(8,128)S(1)} fusion(bf16[2048,640]{1,0:T(8,128)(2,1)} %param.25, f32[2048]{0:T(1024)S(1)} %copy-done.2, f32[128]{0:T(128)S(1)} %add_rsqrt_fusion, bf16[128,2048]{1,0:T(8,128)(2,1)S(1)} %all_gather.3, bf16[128,2048]{1,0:T(8,128)(2,1)} %all-reduce.2.cloned.1.call-done), kind=kOutput, calls=%fused_computation.99 | convolution fusion | flops 337117184 | bytes 4006400 | tf_op jit(solution)/shard_map/dot_general | solution.py:146
  142.9 0.0 copy-start.4
  143.0 3.8 %convolution_convert_fusion.4 = bf16[128,2048]{1,0:T(8,128)(2,1)} fusion(bf16[640,2048]{1,0:T(8,128)(2,1)S(1)} %copy-done, bf16[2048,640]{1,0:T(8,128)(2,1)} %param.26, f32[128,640]{1,0:T(8,128)S(1)} %fusion.52, f32[2048]{0:T(1024)S(1)} %copy-done.2, f32[128]{0:T(128)S(1)} %add_rsqrt_fusion, bf16[128,2048]{1,0:T(8,128)(2,1)S(1)} %all_gather.3, ...), kind=kOutput, calls=%fused_computation.6 | convolution fusion | flops 673415168 | bytes 7152128 | tf_op jit(solution)/shard_map/dot_general | solution.py:150
  146.8 0.0 reduce-scatter.2.cloned.1.call-update
  146.8 24.9 %reduce-scatter.2.cloned.1.call-done = bf16[128,512]{1,0:T(8,128)(2,1)} async-done(((bf16[128,2048]{1,0:T(8,128)(2,1)}), bf16[128,512]{1,0:T(8,128)(2,1)}) %reduce-scatter.2.cloned.1.call-update) | async-done | bytes 131088 | tf_op jit(solution)/shard_map/reduce_scatter | solution.py:151
  171.7 1.0 add_convert_fusion
  172.7 0.1 reshape.209
  172.8 1.5 fusion.1
  174.3 3.4 %reduce.7 = bf16[64,8192]{1,0:T(8,128)(2,1)} reduce(bf16[64,1,8192]{2,0,1:T(8,128)(2,1)} %fusion.1, bf16[]{:T(256)} %broadcast.99), dimensions={1}, to_apply=%copy.87.reduce_sub_computation | reduce | bytes 2097154 | tf_op jit(solution)/shard_map/reshape | solution.py:159
  177.7 2.6 %reshape.221 = bf16[64,2,4096]{2,1,0:T(2,128)(2,1)} reshape(bf16[64,8192]{1,0:T(8,128)(2,1)} %reduce.7) | data formatting | bytes 2097152
  180.3 13.3 %all-to-all-start.1 = ((bf16[64,2,4096]{2,1,0:T(2,128)(2,1)}), bf16[64,2,4096]{2,1,0:T(2,128)(2,1)}, u32[]{:S(2)}, u32[]{:S(2)}) async-start(bf16[64,2,4096]{2,1,0:T(2,128)(2,1)} %reshape.221), calls=%async_computation.2 | async-start | bytes 2097152 | tf_op jit(solution)/shard_map/all_to_all | solution.py:160
  193.7 0.8 fusion.10
  194.5 27.6 %all-to-all-done.1 = bf16[64,2,4096]{2,1,0:T(2,128)(2,1)} async-done(((bf16[64,2,4096]{2,1,0:T(2,128)(2,1)}), bf16[64,2,4096]{2,1,0:T(2,128)(2,1)}, u32[]{:S(2)}, u32[]{:S(2)}) %all-to-all-start.1) | async-done | bytes 1048608 | tf_op jit(solution)/shard_map/all_to_all | solution.py:160
  222.1 7.5 %reshape.222 = bf16[64,1,8192]{2,1,0:T(2,128)(2,1)} reshape(bf16[64,2,4096]{2,1,0:T(2,128)(2,1)} %all-to-all-done.1) | data formatting | bytes 2097152
  229.6 2.8 %convolution_convert_fusion.2 = bf16[8,8192]{1,0:T(8,128)(2,1)S(1)} fusion(bf16[64,1,8192]{2,1,0:T(2,128)(2,1)} %reshape.222, s32[8]{0:T(128)S(1)} %copy-done.6), kind=kOutput, calls=%fused_computation.4 | convolution fusion | flops 8454656 | bytes 1179680 | tf_op jit(solution)/shard_map/dot_general | solution.py:161
  232.4 0.7 copy.88
  (26 shorter events, 0.1 us)
Async XLA Ops:
  7.2 135.8 %copy-start = (bf16[640,2048]{1,0:T(8,128)(2,1)S(1)}, bf16[640,2048]{1,0:T(8,128)(2,1)}, u32[]{:S(2)}) copy-start(bf16[640,2048]{1,0:T(8,128)(2,1)} %param.27) | copy-start | bytes 7864324
  9.5 0.5 copy-start.5
  15.4 16.1 %copy-start.7 = (s32[8,16]{1,0:T(8,128)S(1)}, s32[8,16]{1,0:T(8,128)}, u32[]{:S(2)}) copy-start(s32[8,16]{1,0:T(8,128)} %param.17) | copy-start | bytes 1540
  15.4 17.1 %copy-start.9 = (s32[8]{0:T(128)S(1)}, s32[8]{0:T(128)}, u32[]{:S(2)}) copy-start(s32[8]{0:T(128)} %param.16) | copy-start | bytes 100
  15.4 17.7 %copy-start.8 = (s32[512]{0:T(512)S(1)}, s32[512]{0:T(512)}, u32[]{:S(2)}) copy-start(s32[512]{0:T(512)} %param.15) | copy-start | bytes 6148
  18.1 41.6 %all-to-all-start = ((bf16[64,2,4096]{2,1,0:T(2,128)(2,1)}), bf16[64,2,4096]{2,1,0:T(2,128)(2,1)}, u32[]{:S(2)}, u32[]{:S(2)}) async-start(bf16[64,2,4096]{2,1,0:T(2,128)(2,1)} %reshape.219), calls=%async_computation | async-start | bytes 2097152 | tf_op jit(solution)/shard_map/all_to_all | solution.py:86
  31.3 106.9 %all-reduce.2.cloned.1.call-start = ((), (), s32[]{:S(2)}) async-start(), calls=%async_computation.3 | async-start | bytes 1048576 | tf_op jit(solution)/shard_map/psum | solution.py:141
  33.4 36.6 %copy-start.3 = (bf16[8,64]{1,0:T(8,128)(2,1)}, bf16[8,64]{1,0:T(8,128)(2,1)S(1)}, u32[]{:S(2)}) copy-start(bf16[8,64]{1,0:T(8,128)(2,1)S(1)} %convolution_convert_fusion.8) | copy-start | bytes 3076
  33.4 48.2 %copy-start.10 = (f32[2048]{0:T(1024)S(1)}, f32[2048]{0:T(1024)}, u32[]{:S(2)}) copy-start(f32[2048]{0:T(1024)} %param.20) | copy-start | bytes 24580
  85.4 5.1 %copy-start.1 = (bf16[128,128]{1,0:T(8,128)(2,1)S(1)}, bf16[128,128]{1,0:T(8,128)(2,1)}, u32[]{:S(2)}) copy-start(bf16[128,128]{1,0:T(8,128)(2,1)} %convolution_convert_fusion.6) | copy-start | bytes 98308
  90.5 49.9 %copy-start.2 = (f32[2048]{0:T(1024)S(1)}, f32[2048]{0:T(1024)}, u32[]{:S(2)}) copy-start(f32[2048]{0:T(1024)} %param.24) | copy-start | bytes 24580
  93.2 78.4 %reduce-scatter.2.cloned.1.call-start = ((), (), s32[]{:S(2)}) async-start(), calls=%async_computation.4 | async-start | bytes 655360 | tf_op jit(solution)/shard_map/reduce_scatter | solution.py:151
  142.9 29.8 %copy-start.4 = (bf16[8,64]{1,0:T(8,128)(2,1)S(1)}, bf16[8,64]{1,0:T(8,128)(2,1)}, u32[]{:S(2)}) copy-start(bf16[8,64]{1,0:T(8,128)(2,1)} %copy-done.3) | copy-start | bytes 3076
  177.7 16.0 %copy-start.11 = (s32[8,8]{1,0:T(8,128)S(1)}, s32[8,8]{1,0:T(8,128)}, u32[]{:S(2)}) copy-start(s32[8,8]{1,0:T(8,128)} %param.18) | copy-start | bytes 772
  180.3 49.3 %copy-start.6 = (s32[8]{0:T(128)S(1)}, s32[8]{0:T(128)}, u32[]{:S(2)}) copy-start(s32[8]{0:T(128)} %copy-done.5) | copy-start | bytes 100
  180.3 41.8 %all-to-all-start.1 = ((bf16[64,2,4096]{2,1,0:T(2,128)(2,1)}), bf16[64,2,4096]{2,1,0:T(2,128)(2,1)}, u32[]{:S(2)}, u32[]{:S(2)}) async-start(bf16[64,2,4096]{2,1,0:T(2,128)(2,1)} %reshape.221), calls=%async_computation.2 | async-start | bytes 2097152 | tf_op jit(solution)/shard_map/all_to_all | solution.py:160
Sparse Core Ops, SparseCore 0:
  93.3 44.7 all-reduce.1
  146.9 24.6 reduce-scatter.1
where the time goes:
time: 241 us; the launch traced here: 240 us
  waiting for transfers between devices  124 us (51%)
  matrix products  27.5 us (11%)
  starting transfers between devices  26.6 us (11%)
  local copies, waits for them, and re-layouts  24 us (10%)
  between operations  14.3 us (6%)
  other arithmetic  12.4 us (5%)
  blocking collectives  11.4 us (5%)
    psum x1, waiting for transfers between devices, per_device(): lax.psum(head_part.astype(jnp.bfloat16), 'mlp').astype(jnp.float32)  44.9 us
    all_to_all x1, waiting for transfers between devices, per_device(): lax.all_to_all(returning, 'req', split_axis=0, concat_axis=0, tiled=True)  27.6 us
    all_to_all x1, waiting for transfers between devices, per_device(): lax.all_to_all(outgoing, 'req', split_axis=0, concat_axis=0, tiled=True)  26.3 us
    reduce_scatter x1, waiting for transfers between devices, per_device(): lax.psum_scatter(unit_part.astype(jnp.bfloat16), 'mlp', scatter_dimension...  24.9 us
    unnamed x30, local copies, waits for them, and re-layouts  22.6 us
    all_to_all x1, starting transfers between devices, per_device(): lax.all_to_all(returning, 'req', split_axis=0, concat_axis=0, tiled=True)  13.3 us
    all_to_all x1, starting transfers between devices, per_device(): lax.all_to_all(outgoing, 'req', split_axis=0, concat_axis=0, tiled=True)  13.2 us
    all_gather x1, blocking collectives, per_device(): full_rows = lax.all_gather(local_rows, 'mlp', axis=1, tiled=True)  11.4 us
  transfers between devices with their start and end apart: 4, of which 4 were waited for; matrix products, arithmetic and copies ran while one was open for 1% of the time, Pallas kernels for 0%

commit v1 on v0

--- a/solution.py
+++ b/solution.py
@@ -138,7 +138,9 @@
     )
     attended = attended.reshape(per_owner_rows * tokens, kv_heads * group_heads * HEAD_DIM)
     head_part = jnp.dot(attended, w_out, preferred_element_type=jnp.float32)
-    attn_sum = lax.psum(head_part.astype(jnp.bfloat16), "mlp").astype(jnp.float32)
+    attn_sum = jnp.sum(lax.all_gather(head_part.astype(jnp.bfloat16), "mlp"), axis=0).astype(
+        jnp.float32
+    )
     residual = wide_rows + attn_sum
     normed_two = (
         residual * lax.rsqrt(jnp.mean(residual * residual, axis=1, keepdims=True) + EPS) * mlp_gain

time: 241 us -> 229 us (0.950)
  waiting for transfers between devices: 124 us -> 108 us
  other arithmetic: 12.4 us -> 15.3 us
    psum x1 -> x0, waiting for transfers between devices: 44.9 us -> none  [per_device(): lax.psum(head_part.astype(jnp.bfloat16), 'mlp').astype(jnp.float32)]
    all_gather x0 -> x1, waiting for transfers between devices: none -> 32.1 us  [per_device(): lax.all_gather(head_part.astype(jnp.bfloat16), 'mlp')]
    reduce_sum x0 -> x1, other arithmetic: none -> 2.92 us  [per_device(): jnp.sum(lax.all_gather(head_part.astype(jnp.bfloat16), 'mlp'), axis=0)]
    reduce_scatter x1, waiting for transfers between devices: 24.9 us -> 22.2 us  [per_device(): lax.psum_scatter(unit_part.astype(jnp.bfloat16), 'mlp', scatter_dimension...]
where the time goes in v1:
time: 229 us; the launch traced here: 228 us
  waiting for transfers between devices  108 us (47%)
  matrix products  27.5 us (12%)
  starting transfers between devices  26.8 us (12%)
  local copies, waits for them, and re-layouts  24 us (10%)
  other arithmetic  15.3 us (7%)
  between operations  14.3 us (6%)
  blocking collectives  11.4 us (5%)
    all_gather x1, waiting for transfers between devices, per_device(): lax.all_gather(head_part.astype(jnp.bfloat16), 'mlp')  32.1 us
    all_to_all x1, waiting for transfers between devices, per_device(): lax.all_to_all(returning, 'req', split_axis=0, concat_axis=0, tiled=True)  27.6 us
    all_to_all x1, waiting for transfers between devices, per_device(): lax.all_to_all(outgoing, 'req', split_axis=0, concat_axis=0, tiled=True)  26.3 us
    unnamed x30, local copies, waits for them, and re-layouts  22.6 us
    reduce_scatter x1, waiting for transfers between devices, per_device(): lax.psum_scatter(unit_part.astype(jnp.bfloat16), 'mlp', scatter_dimension...  22.2 us
    all_to_all x1, starting transfers between devices, per_device(): lax.all_to_all(returning, 'req', split_axis=0, concat_axis=0, tiled=True)  13.5 us
    all_to_all x1, starting transfers between devices, per_device(): lax.all_to_all(outgoing, 'req', split_axis=0, concat_axis=0, tiled=True)  13.2 us
    all_gather x1, blocking collectives, per_device(): full_rows = lax.all_gather(local_rows, 'mlp', axis=1, tiled=True)  11.4 us
  transfers between devices with their start and end apart: 4, of which 4 were waited for; matrix products, arithmetic and copies ran while one was open for 1% of the time, Pallas kernels for 0%

profile of v1, /device:TPU:1, one launch (start us, length us, event | category | flops | bytes accessed | tf_op | source)
XLA Modules:
  0.0 227.5 jit_solution(8010673737862079028)
XLA Ops:
  7.2 0.0 copy-start
  7.2 0.8 add_select_fusion
  8.0 0.1 reshape.195
  8.1 0.1 copy.74
  8.2 1.0 copy.100
  9.2 0.1 convert_reduce_fusion.2
  9.3 0.2 add_reduce_fusion
  9.5 0.5 copy-done.5
  10.0 1.4 fusion
  11.4 0.6 broadcast.99
  12.0 3.4 %reduce.7 = bf16[64,8192]{1,0:T(8,128)(2,1)} reduce(bf16[64,1,8192]{2,0,1:T(8,128)(2,1)} %fusion, bf16[]{:T(256)} %broadcast.99), dimensions={1}, to_apply=%copy.78.reduce_sub_computation | reduce | bytes 2097154 | tf_op jit(solution)/shard_map/reshape | solution.py:85
  15.4 2.7 %reshape.220 = bf16[64,2,4096]{2,1,0:T(2,128)(2,1)} reshape(bf16[64,8192]{1,0:T(8,128)(2,1)} %reduce.7) | data formatting | bytes 2097152
  18.1 13.2 %all-to-all-start = ((bf16[64,2,4096]{2,1,0:T(2,128)(2,1)}), bf16[64,2,4096]{2,1,0:T(2,128)(2,1)}, u32[]{:S(2)}, u32[]{:S(2)}) async-start(bf16[64,2,4096]{2,1,0:T(2,128)(2,1)} %reshape.220), calls=%async_computation | async-start | bytes 2097152 | tf_op jit(solution)/shard_map/all_to_all | solution.py:86
  31.3 0.0 all-gather.3.cloned.1.call-start
  31.3 0.1 copy.77
  31.4 0.1 add.93
  31.5 0.0 copy-done.7
  31.5 0.3 convolution_minimum_fusion.3
  31.8 0.2 convolution_minimum_fusion.2
  32.0 0.2 convolution_minimum_fusion.1
  32.2 0.2 fusion.9
  32.4 0.1 copy.82
  32.5 0.7 iota_compare_fusion.10
  33.2 0.3 convolution_convert_fusion.8
  33.4 26.3 %all-to-all-done = bf16[64,2,4096]{2,1,0:T(2,128)(2,1)} async-done(((bf16[64,2,4096]{2,1,0:T(2,128)(2,1)}), bf16[64,2,4096]{2,1,0:T(2,128)(2,1)}, u32[]{:S(2)}, u32[]{:S(2)}) %all-to-all-start) | async-done | bytes 1048608 | tf_op jit(solution)/shard_map/all_to_all | solution.py:86
  59.7 7.5 %reshape.221 = bf16[64,1,8192]{2,1,0:T(2,128)(2,1)} reshape(bf16[64,2,4096]{2,1,0:T(2,128)(2,1)} %all-to-all-done) | data formatting | bytes 2097152
  67.2 2.8 %convolution_convert_fusion.3 = bf16[8,8192]{1,0:T(8,128)(2,1)S(1)} fusion(bf16[8,64]{1,0:T(8,128)(2,1)S(1)} %convolution_convert_fusion.8, bf16[64,1,8192]{2,1,0:T(2,128)(2,1)} %reshape.221), kind=kOutput, calls=%fused_computation.5 | convolution fusion | flops 8454144 | bytes 1180672 | tf_op jit(solution)/shard_map/dot_general | solution.py:87
  70.0 0.1 reshape.199
  70.1 11.4 %all_gather.9 = bf16[128,2048]{1,0:T(8,128)(2,1)S(1)} all-gather(bf16[128,512]{1,0:T(8,128)(2,1)S(1)} %reshape.199), channel_id=1, replica_groups=mesh['req'=64,'mlp'=4] {'mlp'}, dimensions={1}, use_global_device_ids=true | all-gather | bytes 655360 | tf_op jit(solution)/shard_map/all_gather | solution.py:93
  81.4 0.2 fusion.13
  81.6 2.0 convolution_convert_fusion.6
  83.7 1.6 fusion.34
  85.2 0.1 reshape.200
  85.4 0.0 copy-start.1
  85.4 1.5 fusion.53
  86.9 1.8 fusion.54
  88.7 0.3 convert_reduce_fusion
  88.9 1.5 convolution_bitcast_fusion
  90.4 0.1 convert_reduce_fusion.1
  90.5 0.3 fusion.12
  90.8 0.1 copy.86
  90.8 0.1 reshape.208
  91.0 2.2 convolution_convert_fusion.5
  93.2 0.0 all-gather.3.cloned.1.call-update
  93.2 0.0 reduce-scatter.2.cloned.1.call-start
  93.3 32.1 %all-gather.3.cloned.1.call-done = bf16[512,2048]{1,0:T(8,128)(2,1)} async-done(((bf16[128,2048]{1,0:T(8,128)(2,1)}), bf16[512,2048]{1,0:T(8,128)(2,1)}) %all-gather.3.cloned.1.call-update) | async-done | bytes 2097168 | tf_op jit(solution)/shard_map/all_gather | solution.py:141
  125.3 2.9 %reduce_sum.61 = bf16[128,2048]{1,0:T(8,128)(2,1)} reduce(bf16[4,128,2048]{2,1,0:T(8,128)(2,1)} %bitcast.108, bf16[]{:T(256)} %constant.55.clone.1), dimensions={0}, to_apply=%region_6.7 | reduce | flops 786432 | bytes 2621442 | tf_op jit(solution)/shard_map/reduce_sum | solution.py:141
  128.3 2.2 convert_add_fusion
  130.5 2.5 %fusion.52 = f32[128,640]{1,0:T(8,128)S(1)} fusion(bf16[2048,640]{1,0:T(8,128)(2,1)} %param.25, f32[2048]{0:T(1024)S(1)} %copy-done.2, f32[128]{0:T(128)S(1)} %add_rsqrt_fusion, bf16[128,2048]{1,0:T(8,128)(2,1)S(1)} %all_gather.9, bf16[128,2048]{1,0:T(8,128)(2,1)} %reduce_sum.61), kind=kOutput, calls=%fused_computation.99 | convolution fusion | flops 337117184 | bytes 4006400 | tf_op jit(solution)/shard_map/dot_general | solution.py:148
  133.0 0.0 copy-start.4
  133.0 3.8 %convolution_convert_fusion.4 = bf16[128,2048]{1,0:T(8,128)(2,1)} fusion(bf16[640,2048]{1,0:T(8,128)(2,1)S(1)} %copy-done, bf16[2048,640]{1,0:T(8,128)(2,1)} %param.26, f32[128,640]{1,0:T(8,128)S(1)} %fusion.52, f32[2048]{0:T(1024)S(1)} %copy-done.2, f32[128]{0:T(128)S(1)} %add_rsqrt_fusion, bf16[128,2048]{1,0:T(8,128)(2,1)S(1)} %all_gather.9, ...), kind=kOutput, calls=%fused_computation.6 | convolution fusion | flops 673415168 | bytes 7152128 | tf_op jit(solution)/shard_map/dot_general | solution.py:152
  136.9 0.0 reduce-scatter.2.cloned.1.call-update
  136.9 22.2 %reduce-scatter.2.cloned.1.call-done = bf16[128,512]{1,0:T(8,128)(2,1)} async-done(((bf16[128,2048]{1,0:T(8,128)(2,1)}), bf16[128,512]{1,0:T(8,128)(2,1)}) %reduce-scatter.2.cloned.1.call-update) | async-done | bytes 131088 | tf_op jit(solution)/shard_map/reduce_scatter | solution.py:153
  159.1 1.0 add_convert_fusion
  160.1 0.1 reshape.209
  160.2 1.5 fusion.1
  161.7 3.4 %reduce.8 = bf16[64,8192]{1,0:T(8,128)(2,1)} reduce(bf16[64,1,8192]{2,0,1:T(8,128)(2,1)} %fusion.1, bf16[]{:T(256)} %broadcast.99), dimensions={1}, to_apply=%copy.87.reduce_sub_computation | reduce | bytes 2097154 | tf_op jit(solution)/shard_map/reshape | solution.py:161
  165.1 2.6 %reshape.222 = bf16[64,2,4096]{2,1,0:T(2,128)(2,1)} reshape(bf16[64,8192]{1,0:T(8,128)(2,1)} %reduce.8) | data formatting | bytes 2097152
  167.8 13.5 %all-to-all-start.1 = ((bf16[64,2,4096]{2,1,0:T(2,128)(2,1)}), bf16[64,2,4096]{2,1,0:T(2,128)(2,1)}, u32[]{:S(2)}, u32[]{:S(2)}) async-start(bf16[64,2,4096]{2,1,0:T(2,128)(2,1)} %reshape.222), calls=%async_computation.2 | async-start | bytes 2097152 | tf_op jit(solution)/shard_map/all_to_all | solution.py:162
  181.3 0.8 fusion.10
  182.1 27.6 %all-to-all-done.1 = bf16[64,2,4096]{2,1,0:T(2,128)(2,1)} async-done(((bf16[64,2,4096]{2,1,0:T(2,128)(2,1)}), bf16[64,2,4096]{2,1,0:T(2,128)(2,1)}, u32[]{:S(2)}, u32[]{:S(2)}) %all-to-all-start.1) | async-done | bytes 1048608 | tf_op jit(solution)/shard_map/all_to_all | solution.py:162
  209.7 7.5 %reshape.223 = bf16[64,1,8192]{2,1,0:T(2,128)(2,1)} reshape(bf16[64,2,4096]{2,1,0:T(2,128)(2,1)} %all-to-all-done.1) | data formatting | bytes 2097152
  217.2 2.8 %convolution_convert_fusion.2 = bf16[8,8192]{1,0:T(8,128)(2,1)S(1)} fusion(bf16[64,1,8192]{2,1,0:T(2,128)(2,1)} %reshape.223, s32[8]{0:T(128)S(1)} %copy-done.6), kind=kOutput, calls=%fused_computation.4 | convolution fusion | flops 8454656 | bytes 1179680 | tf_op jit(solution)/shard_map/dot_general | solution.py:163
  220.0 0.7 copy.88
  (27 shorter events, 0.1 us)
Async XLA Ops:
  7.2 125.9 %copy-start = (bf16[640,2048]{1,0:T(8,128)(2,1)S(1)}, bf16[640,2048]{1,0:T(8,128)(2,1)}, u32[]{:S(2)}) copy-start(bf16[640,2048]{1,0:T(8,128)(2,1)} %param.27) | copy-start | bytes 7864324
  9.5 0.5 copy-start.5
  15.4 16.1 %copy-start.7 = (s32[8,16]{1,0:T(8,128)S(1)}, s32[8,16]{1,0:T(8,128)}, u32[]{:S(2)}) copy-start(s32[8,16]{1,0:T(8,128)} %param.17) | copy-start | bytes 1540
  15.4 17.1 %copy-start.9 = (s32[8]{0:T(128)S(1)}, s32[8]{0:T(128)}, u32[]{:S(2)}) copy-start(s32[8]{0:T(128)} %param.16) | copy-start | bytes 100
  15.4 17.7 %copy-start.8 = (s32[512]{0:T(512)S(1)}, s32[512]{0:T(512)}, u32[]{:S(2)}) copy-start(s32[512]{0:T(512)} %param.15) | copy-start | bytes 6148
  18.1 41.6 %all-to-all-start = ((bf16[64,2,4096]{2,1,0:T(2,128)(2,1)}), bf16[64,2,4096]{2,1,0:T(2,128)(2,1)}, u32[]{:S(2)}, u32[]{:S(2)}) async-start(bf16[64,2,4096]{2,1,0:T(2,128)(2,1)} %reshape.220), calls=%async_computation | async-start | bytes 2097152 | tf_op jit(solution)/shard_map/all_to_all | solution.py:86
  31.3 94.1 %all-gather.3.cloned.1.call-start = ((), (), s32[]{:S(2)}) async-start(), calls=%async_computation.4 | async-start | bytes 2621440 | tf_op jit(solution)/shard_map/all_gather | solution.py:141
  33.4 36.6 %copy-start.3 = (bf16[8,64]{1,0:T(8,128)(2,1)}, bf16[8,64]{1,0:T(8,128)(2,1)S(1)}, u32[]{:S(2)}) copy-start(bf16[8,64]{1,0:T(8,128)(2,1)S(1)} %convolution_convert_fusion.8) | copy-start | bytes 3076
  33.4 48.2 %copy-start.10 = (f32[2048]{0:T(1024)S(1)}, f32[2048]{0:T(1024)}, u32[]{:S(2)}) copy-start(f32[2048]{0:T(1024)} %param.20) | copy-start | bytes 24580
  85.4 5.1 %copy-start.1 = (bf16[128,128]{1,0:T(8,128)(2,1)S(1)}, bf16[128,128]{1,0:T(8,128)(2,1)}, u32[]{:S(2)}) copy-start(bf16[128,128]{1,0:T(8,128)(2,1)} %convolution_convert_fusion.6) | copy-start | bytes 98308
  93.2 37.3 %copy-start.2 = (f32[2048]{0:T(1024)S(1)}, f32[2048]{0:T(1024)}, u32[]{:S(2)}) copy-start(f32[2048]{0:T(1024)} %param.24) | copy-start | bytes 24580
  93.2 65.9 %reduce-scatter.2.cloned.1.call-start = ((), (), s32[]{:S(2)}) async-start(), calls=%async_computation.3 | async-start | bytes 655360 | tf_op jit(solution)/shard_map/reduce_scatter | solution.py:153
  133.0 27.2 %copy-start.4 = (bf16[8,64]{1,0:T(8,128)(2,1)S(1)}, bf16[8,64]{1,0:T(8,128)(2,1)}, u32[]{:S(2)}) copy-start(bf16[8,64]{1,0:T(8,128)(2,1)} %copy-done.3) | copy-start | bytes 3076
  165.1 16.2 %copy-start.11 = (s32[8,8]{1,0:T(8,128)S(1)}, s32[8,8]{1,0:T(8,128)}, u32[]{:S(2)}) copy-start(s32[8,8]{1,0:T(8,128)} %param.18) | copy-start | bytes 772
  167.7 49.5 %copy-start.6 = (s32[8]{0:T(128)S(1)}, s32[8]{0:T(128)}, u32[]{:S(2)}) copy-start(s32[8]{0:T(128)} %copy-done.5) | copy-start | bytes 100
  167.8 42.0 %all-to-all-start.1 = ((bf16[64,2,4096]{2,1,0:T(2,128)(2,1)}), bf16[64,2,4096]{2,1,0:T(2,128)(2,1)}, u32[]{:S(2)}, u32[]{:S(2)}) async-start(bf16[64,2,4096]{2,1,0:T(2,128)(2,1)} %reshape.222), calls=%async_computation.2 | async-start | bytes 2097152 | tf_op jit(solution)/shard_map/all_to_all | solution.py:162
Sparse Core Ops, SparseCore 0:
  93.3 31.9 all-gather.2
  137.0 22.0 reduce-scatter.1
